TPU v7x, 256 devices: a whole 4x4x8 slice. The times are simulated.
256 devices in a mesh: row: 16 (over y, x), col: 16 (over z, core).
Axes of the slice: x: 4, y: 4, z: 8, core: 2. Of those that a mesh axis runs over, the one named last changes fastest.
Arguments:
- q_seq: bfloat16 [2048, 6144], P('row', 'col'), may hold values from -4.5 to 4.5
- k_seq: bfloat16 [2048, 6144], P('row', 'col'), may hold values from -4.5 to 4.5
- v_seq: bfloat16 [2048, 6144], P('row', 'col'), may hold values from -6 to 6
- resid: bfloat16 [2048, 6144], P('row', 'col'), may hold values from -90 to 90
- ln_gain: float32 [6144], replicated, may hold values from 0.1 to 1.9
- w_up: bfloat16 [6144, 24576], P('row', 'col'), may hold values from -0.078125 to 0.078125
Outputs:
- hidden: bfloat16 [2048, 24576], P('row', 'col')
All inputs are finite; a program needn't handle non-finite values.
Results may differ from a plain program's by a relative error of at most 0.0051.
Values may be sent and summed in bfloat16 or wider, within the bound.
No kernel may reach another device: no remote copies, remote signals or barrier semaphores. Data moves between devices by JAX's collectives and lax.ppermute only.
A program may use at most 64 MiB of HBM per device.

v0:
```python
import math
import jax
import jax.numpy as jnp
from jax import lax
from jax.sharding import Mesh, PartitionSpec as P

HD = 128


def attention_block(query, keys, values):
    seq, width = query.shape
    heads = width // HD
    qshaped = query.reshape(seq, heads, HD)
    kshaped = keys.reshape(seq, heads, HD)
    vshaped = values.reshape(seq, heads, HD)
    scores = jnp.einsum("qhd,khd->hqk", qshaped, kshaped, preferred_element_type=jnp.float32)
    scores = scores * (1.0 / math.sqrt(HD))
    rows_idx = lax.broadcasted_iota(jnp.int32, (seq, seq), 0)
    cols_idx = lax.broadcasted_iota(jnp.int32, (seq, seq), 1)
    scores = jnp.where((rows_idx >= cols_idx)[None], scores, -1e30)
    highest = jnp.max(scores, axis=-1, keepdims=True)
    expo = jnp.exp(scores - highest)
    prob = (expo / jnp.sum(expo, axis=-1, keepdims=True)).astype(jnp.bfloat16)
    output = jnp.einsum("hqk,khd->qhd", prob, vshaped, preferred_element_type=jnp.float32)
    return output.astype(jnp.bfloat16).reshape(seq, width)


def per_device(q_seq, k_seq, v_seq, resid, ln_gain, w_up):
    w_group = lax.all_gather(w_up, "rx", axis=0, tiled=True)
    res_tokens = lax.all_to_all(resid, "col", split_axis=0, concat_axis=1, tiled=True)
    attended = attention_block(q_seq, k_seq, v_seq)
    att_tokens = lax.all_to_all(attended, "col", split_axis=0, concat_axis=1, tiled=True)
    stream = res_tokens.astype(jnp.float32) + att_tokens.astype(jnp.float32)
    full_width = stream.shape[1]
    mean = jnp.sum(stream, axis=1, keepdims=True) / full_width
    spread = jnp.sum(stream * stream, axis=1, keepdims=True) / full_width - mean * mean
    normed = ((stream - mean) * lax.rsqrt(spread + 1e-05) * ln_gain[None, :]).astype(jnp.bfloat16)
    part = lax.all_to_all(normed, "ry", split_axis=1, concat_axis=0, tiled=True)
    n_y = part.shape[0] // normed.shape[0]
    part = part.reshape(n_y, normed.shape[0], part.shape[1])
    tokens = lax.all_gather(part, "col", axis=0, tiled=False)
    partial = jnp.einsum("cytf,fu->yctu", tokens, w_group, preferred_element_type=jnp.float32)
    partial = partial.reshape(-1, partial.shape[-1])
    product = lax.psum_scatter(partial, "ry", scatter_dimension=0, tiled=True)
    return jax.nn.gelu(product, approximate=True).astype(jnp.bfloat16)


def solution(mesh):
    n_row, n_col = (mesh.shape["row"], mesh.shape["col"])
    nx = len({d.coords[0] for d in mesh.devices[:, 0]})
    split = Mesh(mesh.devices.reshape(n_row // nx, nx, n_col), ("ry", "rx", "col"))
    rows = ("ry", "rx")
    placed = (P(rows, "col"), P(rows, "col"), P(rows, "col"), P(rows, "col"), P(), P(rows, "col"))

    def body(q_seq, k_seq, v_seq, resid, ln_gain, w_up):
        return per_device(q_seq, k_seq, v_seq, resid, ln_gain, w_up)

    return jax.shard_map(
        body, mesh=split, in_specs=placed, out_specs=P(rows, "col"), check_vma=False
    )
```

profile of v0, /device:TPU:1, one launch (start us, length us, event | category | flops | bytes accessed | tf_op | source)
XLA Modules:
  0.0 193.7 jit_solution(17831639695960104614)
XLA Ops:
  6.5 10.0 %all-to-all-start = ((bf16[16,8,384]{2,1,0:T(8,128)(2,1)}), bf16[16,8,384]{2,1,0:T(8,128)(2,1)S(1)}, u32[]{:S(2)}, u32[]{:S(2)}) async-start(bf16[16,8,384]{2,1,0:T(8,128)(2,1)} %bitcast.32), calls=%async_computation | async-start | bytes 196608 | tf_op jit(solution)/shard_map/all_to_all | solution.py:30
  16.5 1.0 copy.20
  17.6 1.0 copy.21
  18.6 0.2 fusion.7
  18.8 0.1 fusion.21
  18.9 1.0 copy.24
  19.9 0.3 fusion.9
  20.2 0.1 copy.27
  20.2 0.7 all_to_all.32
  21.0 4.0 %all-to-all-done = bf16[16,8,384]{2,1,0:T(8,128)(2,1)S(1)} async-done(((bf16[16,8,384]{2,1,0:T(8,128)(2,1)}), bf16[16,8,384]{2,1,0:T(8,128)(2,1)S(1)}, u32[]{:S(2)}, u32[]{:S(2)}) %all-to-all-start) | async-done | bytes 98336 | tf_op jit(solution)/shard_map/all_to_all | solution.py:30
  25.0 3.4 %all-to-all-start.1 = ((bf16[16,8,384]{2,1,0:T(8,128)(2,1)}), bf16[16,8,384]{2,1,0:T(8,128)(2,1)S(1)}, u32[]{:S(2)}, u32[]{:S(2)}) async-start(bf16[16,8,384]{2,1,0:T(8,128)(2,1)} %all_to_all.32), calls=%async_computation.1 | async-start | bytes 196608 | tf_op jit(solution)/shard_map/all_to_all | solution.py:32
  28.4 0.0 all-gather.6.cloned.1.call-start
  28.5 0.8 mul.66
  29.2 7.5 %all-to-all-done.1 = bf16[16,8,384]{2,1,0:T(8,128)(2,1)S(1)} async-done(((bf16[16,8,384]{2,1,0:T(8,128)(2,1)}), bf16[16,8,384]{2,1,0:T(8,128)(2,1)S(1)}, u32[]{:S(2)}, u32[]{:S(2)}) %all-to-all-start.1) | async-done | bytes 98336 | tf_op jit(solution)/shard_map/all_to_all | solution.py:32
  36.8 0.2 fusion.20
  37.0 0.1 multiply_convert_fusion
  37.1 8.8 %all_to_all.39 = bf16[8,4,1536]{2,0,1:T(8,128)(2,1)} all-to-all(bf16[8,4,1536]{2,0,1:T(8,128)(2,1)S(1)} %multiply_convert_fusion), channel_id=1, replica_groups=mesh['ry'=4,'rx'=4,'col'=16] {'ry'}, dimensions={1} | all-to-all | bytes 196608 | tf_op jit(solution)/shard_map/all_to_all | solution.py:38
  45.9 0.7 all-gather.4.cloned.1.call-update
  46.7 34.7 %all-gather.6.cloned.1.call-done = bf16[64,8,1536]{2,1,0:T(8,128)(2,1)} async-done(((bf16[4,8,1536]{2,1,0:T(8,128)(2,1)}), bf16[64,8,1536]{2,1,0:T(8,128)(2,1)}) %all-gather.6.cloned.1.call-update) | async-done | bytes 1572880 | tf_op jit(solution)/shard_map/all_gather | solution.py:41
  81.4 55.2 %all-gather.4.cloned.1.call-done = bf16[1536,1536]{1,0:T(8,128)(2,1)} async-done(((bf16[384,1536]{1,0:T(8,128)(2,1)}), bf16[1536,1536]{1,0:T(8,128)(2,1)}) %all-gather.4.cloned.1.call-update) | async-done | bytes 4718608 | tf_op jit(solution)/shard_map/all_gather | solution.py:29
  136.6 4.9 %fusion.3 = f32[4,16,8,1536]{3,2,0,1:T(8,128)S(1)} fusion(bf16[16,4,8,1536]{3,2,1,0:T(8,128)(2,1)} %bitcast.34, bf16[1536,1536]{1,0:T(8,128)(2,1)} %all-gather.4.cloned.1.call-done), kind=kOutput, calls=%fused_computation.3 | convolution fusion | flops 2415919104 | bytes 9437184 | tf_op jit(solution)/shard_map/cytf,fu->yctu/dot_general | solution.py:42
  141.6 1.9 copy.28
  143.5 41.5 %reduce-scatter.2.cloned.1.call-done = f32[128,1536]{1,0:T(8,128)} async-done(((f32[512,1536]{1,0:T(8,128)}), f32[128,1536]{1,0:T(8,128)}) %reduce-scatter.2.cloned.1.call-update) | async-done | bytes 786448 | tf_op jit(solution)/shard_map/reduce_scatter | solution.py:44
  185.0 2.1 %fusion.17 = bf16[128,1536]{1,0:T(8,128)(2,1)} fusion(f32[128,1536]{1,0:T(8,128)} %reduce-scatter.2.cloned.1.call-done), kind=kLoop, calls=%fused_computation.18 | loop fusion | flops 1769472 | bytes 1179648 | tf_op jit(solution)/shard_map/convert_element_type | solution.py:45
  (6 shorter events, 0.1 us)
Async XLA Ops:
  6.5 18.5 %all-to-all-start = ((bf16[16,8,384]{2,1,0:T(8,128)(2,1)}), bf16[16,8,384]{2,1,0:T(8,128)(2,1)S(1)}, u32[]{:S(2)}, u32[]{:S(2)}) async-start(bf16[16,8,384]{2,1,0:T(8,128)(2,1)} %bitcast.32), calls=%async_computation | async-start | bytes 196608 | tf_op jit(solution)/shard_map/all_to_all | solution.py:30
  25.0 11.8 %all-to-all-start.1 = ((bf16[16,8,384]{2,1,0:T(8,128)(2,1)}), bf16[16,8,384]{2,1,0:T(8,128)(2,1)S(1)}, u32[]{:S(2)}, u32[]{:S(2)}) async-start(bf16[16,8,384]{2,1,0:T(8,128)(2,1)} %all_to_all.32), calls=%async_computation.1 | async-start | bytes 196608 | tf_op jit(solution)/shard_map/all_to_all | solution.py:32
  28.4 53.0 %all-gather.6.cloned.1.call-start = ((), (), s32[]{:S(2)}) async-start(), calls=%async_computation.6 | async-start | bytes 1671168 | tf_op jit(solution)/shard_map/all_gather | solution.py:41
  45.9 90.8 %all-gather.4.cloned.1.call-start = ((), (), s32[]{:S(2)}) async-start(), calls=%async_computation.4 | async-start | bytes 5898240 | tf_op jit(solution)/shard_map/all_gather | solution.py:29
  46.6 138.4 %reduce-scatter.2.cloned.1.call-start = ((), (), s32[]{:S(2)}) async-start(), calls=%async_computation.5 | async-start | bytes 3932160 | tf_op jit(solution)/shard_map/reduce_scatter | solution.py:44
Sparse Core Ops, SparseCore 0:
  46.0 35.3 all-gather.5
  83.2 53.3 all-gather.3
  143.6 41.3 reduce-scatter.1
where the time goes:
time: 194 us
  waiting for transfers between devices  144 us (74%)
  starting transfers between devices  13.5 us (7%)
  between operations  13.2 us (7%)
  blocking collectives  8.75 us (5%)
  local copies, waits for them, and re-layouts  6.52 us (3%)
  matrix products  5.43 us (3%)
  other arithmetic  2.53 us (1%)
    all_gather x1, waiting for transfers between devices, per_device(): w_group = lax.all_gather(w_up, 'rx', axis=0, tiled=True)  55.2 us
    reduce_scatter x1, waiting for transfers between devices, per_device(): product = lax.psum_scatter(partial, 'ry', scatter_dimension=0, tiled=True)  41.5 us
    all_gather x1, waiting for transfers between devices, per_device(): tokens = lax.all_gather(part, 'col', axis=0, tiled=False)  34.7 us
    all_to_all x1, starting transfers between devices, per_device(): lax.all_to_all(resid, 'col', split_axis=0, concat_axis=1, tiled=True)  9.98 us
    all_to_all x1, blocking collectives, per_device(): part = lax.all_to_all(normed, 'ry', split_axis=1, concat_axis=0, tiled=True)  8.75 us
    all_to_all x1, waiting for transfers between devices, per_device(): lax.all_to_all(attended, 'col', split_axis=0, concat_axis=1, tiled=True)  7.54 us
    dot_general x1, matrix products, per_device(): jnp.einsum('cytf,fu->yctu', tokens, w_group, preferred_element_type=jnp.f...  4.94 us
    all_to_all x1, waiting for transfers between devices, per_device(): lax.all_to_all(resid, 'col', split_axis=0, concat_axis=1, tiled=True)  4.03 us
  transfers between devices with their start and end apart: 5, of which 5 were waited for; matrix products, arithmetic and copies ran while one was open for 2% of the time, Pallas kernels for 0%

commit v1 on v0

--- a/solution.py
+++ b/solution.py
@@ -26,7 +26,8 @@
 
 
 def per_device(q_seq, k_seq, v_seq, resid, ln_gain, w_up):
-    w_group = lax.all_gather(w_up, "rx", axis=0, tiled=True)
+    outgoing = jnp.stack([w_up] * lax.axis_size("rx"))
+    w_group = jnp.concatenate(lax.all_to_all(outgoing, "rx", 0, 0), axis=0)
     res_tokens = lax.all_to_all(resid, "col", split_axis=0, concat_axis=1, tiled=True)
     attended = attention_block(q_seq, k_seq, v_seq)
     att_tokens = lax.all_to_all(attended, "col", split_axis=0, concat_axis=1, tiled=True)

time: 194 us -> 158 us (0.81)
  waiting for transfers between devices: 144 us -> 100 us
  starting transfers between devices: 13.5 us -> 18.5 us
  local copies, waits for them, and re-layouts: 6.52 us -> 9.06 us
    all_gather x1 -> x0, waiting for transfers between devices: 55.2 us -> none  [per_device(): w_group = lax.all_gather(w_up, 'rx', axis=0, tiled=True)]
    all_to_all x0 -> x1, waiting for transfers between devices: none -> 14.8 us  [per_device(): w_group = jnp.concatenate(lax.all_to_all(outgoing, 'rx', 0, 0), axis=0)]
    reduce_scatter x1, waiting for transfers between devices: 41.5 us -> 35.5 us  [per_device(): product = lax.psum_scatter(partial, 'ry', scatter_dimension=0, tiled=True)]
    all_to_all x0 -> x1, starting transfers between devices: none -> 4.93 us  [per_device(): w_group = jnp.concatenate(lax.all_to_all(outgoing, 'rx', 0, 0), axis=0)]
    all_gather x1, waiting for transfers between devices: 34.7 us -> 37.6 us  [per_device(): tokens = lax.all_gather(part, 'col', axis=0, tiled=False)]
    another operation x0 -> x1, local copies, waits for them, and re-layouts: none -> 2.54 us  [per_device(): outgoing = jnp.stack([w_up] * lax.axis_size('rx'))]
  transfers between devices with their start and end apart: 5 -> 5, of which waited for: 5 -> 5; matrix products, arithmetic and copies ran while one was open for 2% -> 3% of each run, Pallas kernels for 0% -> 0%
where the time goes in v1:
time: 158 us
  waiting for transfers between devices  100 us (63%)
  starting transfers between devices  18.5 us (12%)
  between operations  13.5 us (9%)
  local copies, waits for them, and re-layouts  9.06 us (6%)
  blocking collectives  8.75 us (6%)
  matrix products  5.42 us (3%)
  other arithmetic  2.53 us (2%)
    all_gather x1, waiting for transfers between devices, per_device(): tokens = lax.all_gather(part, 'col', axis=0, tiled=False)  37.6 us
    reduce_scatter x1, waiting for transfers between devices, per_device(): product = lax.psum_scatter(partial, 'ry', scatter_dimension=0, tiled=True)  35.5 us
    all_to_all x1, waiting for transfers between devices, per_device(): w_group = jnp.concatenate(lax.all_to_all(outgoing, 'rx', 0, 0), axis=0)  14.8 us
    all_to_all x1, starting transfers between devices, per_device(): lax.all_to_all(resid, 'col', split_axis=0, concat_axis=1, tiled=True)  10.1 us
    all_to_all x1, blocking collectives, per_device(): part = lax.all_to_all(normed, 'ry', split_axis=1, concat_axis=0, tiled=True)  8.75 us
    all_to_all x1, waiting for transfers between devices, per_device(): lax.all_to_all(attended, 'col', split_axis=0, concat_axis=1, tiled=True)  7.59 us
    dot_general x1, matrix products, per_device(): jnp.einsum('cytf,fu->yctu', tokens, w_group, preferred_element_type=jnp.f...  4.94 us
    all_to_all x1, starting transfers between devices, per_device(): w_group = jnp.concatenate(lax.all_to_all(outgoing, 'rx', 0, 0), axis=0)  4.93 us
  transfers between devices with their start and end apart: 5, of which 5 were waited for; matrix products, arithmetic and copies ran while one was open for 3% of the time, Pallas kernels for 0%

profile of v1, /device:TPU:1, one launch (start us, length us, event | category | flops | bytes accessed | tf_op | source)
XLA Modules:
  0.0 157.9 jit_solution(7271602745772196043)
XLA Ops:
  6.5 10.1 %all-to-all-start = ((bf16[16,8,384]{2,1,0:T(8,128)(2,1)}), bf16[16,8,384]{2,1,0:T(8,128)(2,1)S(1)}, u32[]{:S(2)}, u32[]{:S(2)}) async-start(bf16[16,8,384]{2,1,0:T(8,128)(2,1)} %bitcast.31), calls=%async_computation | async-start | bytes 196608 | tf_op jit(solution)/shard_map/all_to_all | solution.py:31
  16.7 1.0 copy.20
  17.7 1.0 copy.21
  18.7 0.2 fusion.2
  19.0 1.0 copy.24
  20.0 0.3 fusion.4
  20.3 0.1 copy.27
  20.4 0.7 all_to_all.35
  21.1 4.0 %all-to-all-done = bf16[16,8,384]{2,1,0:T(8,128)(2,1)S(1)} async-done(((bf16[16,8,384]{2,1,0:T(8,128)(2,1)}), bf16[16,8,384]{2,1,0:T(8,128)(2,1)S(1)}, u32[]{:S(2)}, u32[]{:S(2)}) %all-to-all-start) | async-done | bytes 98336 | tf_op jit(solution)/shard_map/all_to_all | solution.py:31
  25.1 3.4 %all-to-all-start.1 = ((bf16[16,8,384]{2,1,0:T(8,128)(2,1)}), bf16[16,8,384]{2,1,0:T(8,128)(2,1)S(1)}, u32[]{:S(2)}, u32[]{:S(2)}) async-start(bf16[16,8,384]{2,1,0:T(8,128)(2,1)} %all_to_all.35), calls=%async_computation.1 | async-start | bytes 196608 | tf_op jit(solution)/shard_map/all_to_all | solution.py:33
  28.6 0.8 mul.66
  29.3 7.6 %all-to-all-done.1 = bf16[16,8,384]{2,1,0:T(8,128)(2,1)S(1)} async-done(((bf16[16,8,384]{2,1,0:T(8,128)(2,1)}), bf16[16,8,384]{2,1,0:T(8,128)(2,1)S(1)}, u32[]{:S(2)}, u32[]{:S(2)}) %all-to-all-start.1) | async-done | bytes 98336 | tf_op jit(solution)/shard_map/all_to_all | solution.py:33
  36.9 0.2 fusion.15
  37.1 0.1 multiply_convert_fusion
  37.2 8.8 %all_to_all.44 = bf16[8,4,1536]{2,0,1:T(8,128)(2,1)} all-to-all(bf16[8,4,1536]{2,0,1:T(8,128)(2,1)S(1)} %multiply_convert_fusion), channel_id=1, replica_groups=mesh['ry'=4,'rx'=4,'col'=16] {'ry'}, dimensions={1} | all-to-all | bytes 196608 | tf_op jit(solution)/shard_map/all_to_all | solution.py:39
  46.0 2.5 %stack.2 = bf16[4,384,1536]{2,1,0:T(8,128)(2,1)} broadcast(bf16[384,1536]{1,0:T(8,128)(2,1)S(1)} %copy-done), dimensions={1,2} | broadcast | bytes 5898240 | tf_op jit(solution)/shard_map/stack | solution.py:29
  48.5 4.9 %all-to-all-start.3 = ((bf16[4,384,1536]{2,1,0:T(8,128)(2,1)}), bf16[4,384,1536]{2,1,0:T(8,128)(2,1)}, u32[]{:S(2)}, u32[]{:S(2)}) async-start(bf16[4,384,1536]{2,1,0:T(8,128)(2,1)} %stack.2), calls=%async_computation.3 | async-start | bytes 9437184 | tf_op jit(solution)/shard_map/all_to_all | solution.py:30
  53.5 0.7 all-gather.3.cloned.1.call-update
  54.2 37.6 %all-gather.3.cloned.1.call-done = bf16[64,8,1536]{2,1,0:T(8,128)(2,1)} async-done(((bf16[4,8,1536]{2,1,0:T(8,128)(2,1)}), bf16[64,8,1536]{2,1,0:T(8,128)(2,1)}) %all-gather.3.cloned.1.call-update) | async-done | bytes 1572880 | tf_op jit(solution)/shard_map/all_gather | solution.py:42
  91.8 14.8 %all-to-all-done.3 = bf16[4,384,1536]{2,1,0:T(8,128)(2,1)} async-done(((bf16[4,384,1536]{2,1,0:T(8,128)(2,1)}), bf16[4,384,1536]{2,1,0:T(8,128)(2,1)}, u32[]{:S(2)}, u32[]{:S(2)}) %all-to-all-start.3) | async-done | bytes 4718624 | tf_op jit(solution)/shard_map/all_to_all | solution.py:30
  106.6 4.9 %convolution_bitcast_fusion = f32[4,16,8,1536]{3,2,0,1:T(8,128)S(1)} fusion(bf16[16,4,8,1536]{3,2,1,0:T(8,128)(2,1)} %bitcast.33, bf16[1536,1536,1,1]{1,0,3,2:T(8,128)(2,1)} %bitcast.11), kind=kOutput, calls=%fused_computation.1 | convolution fusion | flops 2415919104 | bytes 9437184 | tf_op jit(solution)/shard_map/cytf,fu->yctu/dot_general | solution.py:43
  111.5 1.9 %copy.28 = f32[4,16,8,1536]{3,2,1,0:T(8,128)} copy(f32[4,16,8,1536]{3,2,0,1:T(8,128)S(1)} %convolution_bitcast_fusion) | data formatting | bytes 6291456 | tf_op jit(solution)/shard_map/cytf,fu->yctu/transpose | solution.py:43
  113.5 35.5 %reduce-scatter.2.cloned.1.call-done = f32[128,1536]{1,0:T(8,128)} async-done(((f32[512,1536]{1,0:T(8,128)}), f32[128,1536]{1,0:T(8,128)}) %reduce-scatter.2.cloned.1.call-update) | async-done | bytes 786448 | tf_op jit(solution)/shard_map/reduce_scatter | solution.py:45
  149.0 2.1 %fusion.12 = bf16[128,1536]{1,0:T(8,128)(2,1)} fusion(f32[128,1536]{1,0:T(8,128)} %reduce-scatter.2.cloned.1.call-done), kind=kLoop, calls=%fused_computation.16 | loop fusion | flops 1769472 | bytes 1179648 | tf_op jit(solution)/shard_map/convert_element_type | solution.py:46
  (8 shorter events, 0.2 us)
Async XLA Ops:
  6.5 39.4 %copy-start = (bf16[384,1536]{1,0:T(8,128)(2,1)S(1)}, bf16[384,1536]{1,0:T(8,128)(2,1)}, u32[]{:S(2)}) copy-start(bf16[384,1536]{1,0:T(8,128)(2,1)} %param.11) | copy-start | bytes 3538948
  6.5 18.6 %all-to-all-start = ((bf16[16,8,384]{2,1,0:T(8,128)(2,1)}), bf16[16,8,384]{2,1,0:T(8,128)(2,1)S(1)}, u32[]{:S(2)}, u32[]{:S(2)}) async-start(bf16[16,8,384]{2,1,0:T(8,128)(2,1)} %bitcast.31), calls=%async_computation | async-start | bytes 196608 | tf_op jit(solution)/shard_map/all_to_all | solution.py:31
  25.1 11.8 %all-to-all-start.1 = ((bf16[16,8,384]{2,1,0:T(8,128)(2,1)}), bf16[16,8,384]{2,1,0:T(8,128)(2,1)S(1)}, u32[]{:S(2)}, u32[]{:S(2)}) async-start(bf16[16,8,384]{2,1,0:T(8,128)(2,1)} %all_to_all.35), calls=%async_computation.1 | async-start | bytes 196608 | tf_op jit(solution)/shard_map/all_to_all | solution.py:33
  48.5 58.1 %all-to-all-start.3 = ((bf16[4,384,1536]{2,1,0:T(8,128)(2,1)}), bf16[4,384,1536]{2,1,0:T(8,128)(2,1)}, u32[]{:S(2)}, u32[]{:S(2)}) async-start(bf16[4,384,1536]{2,1,0:T(8,128)(2,1)} %stack.2), calls=%async_computation.3 | async-start | bytes 9437184 | tf_op jit(solution)/shard_map/all_to_all | solution.py:30
  53.4 38.3 %all-gather.3.cloned.1.call-start = ((), (), s32[]{:S(2)}) async-start(), calls=%async_computation.6 | async-start | bytes 1671168 | tf_op jit(solution)/shard_map/all_gather | solution.py:42
  54.2 94.8 %reduce-scatter.2.cloned.1.call-start = ((), (), s32[]{:S(2)}) async-start(), calls=%async_computation.5 | async-start | bytes 3932160 | tf_op jit(solution)/shard_map/reduce_scatter | solution.py:45
Sparse Core Ops, SparseCore 0:
  56.1 35.6 all-gather.2
  113.6 35.3 reduce-scatter.1
